TPU v7x, 256 devices: a whole 4x4x8 slice. The times are simulated.
256 devices in a mesh: tiles: 64 (over y, z, core), cols: 4 (over x).
Axes of the slice: x: 4, y: 4, z: 8, core: 2. Of those that a mesh axis runs over, the one named last changes fastest.
Arguments:
- cov_blocks: bfloat16 [1024, 8, 256, 256], P('tiles', None, 'cols'), may hold values from -1 to 5, as said below
- neighbours: int32 [1024, 8], P('tiles'), may hold values from 0 to 1023, as said below
- voxel_mask: int32 [1024, 256], P('tiles', 'cols'), may hold values 0 or 1
- start_block: bfloat16 [128, 1024, 256], P('cols', 'tiles'), may hold values from -6 to 6
- overdensity: float32 [1024, 256], P('tiles', 'cols'), may hold values from -12 to 12
Outputs:
- basis_next: bfloat16 [128, 1024, 256], P('cols', 'tiles')
- coeffs: float32 [3, 128], replicated
Inputs may be any that keep to these rules, and one draw needn't show every extreme that they name: Slot 0 names the tile itself. Every other entry names another tile at most 3 away, counting cyclically (tile 1024 - 1 is next to tile 0), and some entry is exactly 3 away. If neighbours[i, k] = j then neighbours[j, k] = i. cov_blocks[j, k] is the transpose of cov_blocks[i, k] where neighbours[i, k] = j; the blocks of slot 0 are symmetric.
All inputs are finite; a program needn't handle non-finite values. No bound on the sum of `voxel_mask` on one device may be relied on, other than what follows from the above.
Results may differ from a plain program's by a relative error of at most 0.01.
The roundings to bfloat16 on the way count: a program that leaves them out, or rounds other values in their place, can miss the bound.
Values may be sent and summed in bfloat16 or wider, within the bound.
No kernel may reach another device: no remote copies, remote signals or barrier semaphores. Data moves between devices by JAX's collectives and lax.ppermute only.
A program may use at most 64 MiB of HBM per device.

v0:
```python
import math
import jax
import jax.numpy as jnp
from jax import lax
from jax.sharding import PartitionSpec as P

REACH = 3


def with_halo(cells, sides, width):
    for axis, dim in sides:
        count = lax.axis_size(axis)
        head = lax.slice_in_dim(cells, 0, width, axis=dim)
        tail = lax.slice_in_dim(cells, cells.shape[dim] - width, cells.shape[dim], axis=dim)
        cells = jnp.concatenate(
            [
                lax.ppermute(tail, axis, [(i, (i + 1) % count) for i in range(count)]),
                cells,
                lax.ppermute(head, axis, [((i + 1) % count, i) for i in range(count)]),
            ],
            axis=dim,
        )
    return cells


def orthonormal(work):
    gram = lax.psum(jnp.dot(work, work.T, preferred_element_type=jnp.float32), ("tiles", "cols"))
    lower = jnp.linalg.cholesky(gram)
    identity = jnp.eye(work.shape[0], dtype=jnp.float32)
    inverse = jax.scipy.linalg.solve_triangular(lower, identity, lower=True).astype(jnp.bfloat16)
    return jnp.dot(inverse, work, preferred_element_type=jnp.float32)


def projection(basis_flat, density):
    return jnp.sum(basis_flat.astype(jnp.float32) * density[None, :], axis=1)


def settle(terms):
    return lax.psum(terms, ("tiles", "cols"))


def fold_slots(total, piece, cov_blocks, local_index):
    for slot in range(cov_blocks.shape[1]):
        picked = jnp.take(piece, local_index[:, slot], axis=1)
        blocks = cov_blocks[:, slot]
        total = total + jnp.einsum(
            "iuv,biv->biu", blocks, picked, preferred_element_type=jnp.float32
        )
    return total


def local(cov_blocks, neighbours, voxel_mask, start_block, overdensity):
    tiles_here = neighbours.shape[0]
    voxels_here = voxel_mask.shape[1]
    voxels_all = cov_blocks.shape[3]
    cycle_size = tiles_here * lax.axis_size("tiles")
    first_tile = lax.axis_index("tiles") * tiles_here
    local_index = jnp.mod(neighbours - first_tile + REACH, cycle_size)
    mask_values = voxel_mask.astype(jnp.float32)
    density = overdensity.reshape(-1)
    start_cube = lax.all_to_all(start_block, "cols", split_axis=2, concat_axis=0, tiled=True)
    count = start_cube.shape[0]
    start_flat = (
        (start_cube.astype(jnp.float32) * mask_values[None]).astype(jnp.bfloat16).reshape(count, -1)
    )
    basis_now = orthonormal(start_flat).astype(jnp.bfloat16)
    basis_old = None
    found = []
    pending = projection(basis_now, density)
    found.append(settle(pending))
    rotated = None
    for lanczos_round in range(2):
        image_count = basis_now.shape[0]
        basis_cube = basis_now.reshape(image_count, tiles_here, voxels_here)
        empty = jnp.zeros((image_count, tiles_here, voxels_here), jnp.float32)
        gathered = lax.all_gather(basis_cube, "cols", axis=2, tiled=True)
        padded = with_halo(gathered, (("tiles", 1),), REACH)
        total = fold_slots(empty, padded, cov_blocks, local_index)
        image = (total * mask_values[None]).astype(jnp.bfloat16).reshape(image_count, -1)
        if basis_old is None:
            stacked = basis_now
        else:
            stacked = jnp.concatenate([basis_now, basis_old], axis=0)
        local_sums = jnp.dot(stacked, image.T, preferred_element_type=jnp.float32)
        sums = lax.psum(local_sums, ("tiles", "cols"))
        along = sums[:count].astype(jnp.bfloat16)
        resid = image.astype(jnp.float32) - jnp.dot(
            along.T, basis_now, preferred_element_type=jnp.float32
        )
        if basis_old is not None:
            back = sums[count:].astype(jnp.bfloat16)
            resid = resid - jnp.dot(back.T, basis_old, preferred_element_type=jnp.float32)
        rotated = orthonormal(resid.astype(jnp.bfloat16))
        basis_old, basis_now = (basis_now, rotated.astype(jnp.bfloat16))
        pending = projection(basis_now, density)
        found.append(settle(pending))
    coeffs = jnp.stack(found)
    scaled = (rotated * math.sqrt(cycle_size * voxels_all)).astype(jnp.bfloat16)
    scaled = scaled.reshape(count, tiles_here, voxels_here)
    basis_next = lax.all_to_all(scaled, "cols", split_axis=0, concat_axis=2, tiled=True)
    return (basis_next, coeffs)


def solution(mesh):
    return jax.shard_map(
        local,
        mesh=mesh,
        in_specs=(
            P("tiles", None, "cols", None),
            P("tiles", None),
            P("tiles", "cols"),
            P("cols", "tiles", None),
            P("tiles", "cols"),
        ),
        out_specs=(P("cols", "tiles", None), P()),
        check_vma=False,
    )
```

profile of v0, /device:TPU:1, one launch (start us, length us, event | category | flops | bytes accessed | tf_op | source)
XLA Modules:
  0.0 1190.3 jit_solution(6091634544763093636)
XLA Ops:
  7.2 2.4 copy.138
  9.5 1.7 reshape.230
  11.2 4.8 all-to-all-start
  16.7 4.8 all-to-all-done
  24.7 244.0 %all-reduce.6.cloned.1.call-done = f32[128,128]{0,1:T(8,128)} async-done(((f32[128,128]{0,1:T(8,128)}), f32[128,128]{0,1:T(8,128)}) %all-reduce.6.cloned.1.call-update) | async-done | bytes 65552 | tf_op jit(solution)/shard_map/psum | solution.py:27
  270.5 11.7 cholesky.59
  283.5 9.8 custom-call.7
  295.1 20.7 %all-gather.3.cloned.1.call-done = bf16[128,16,256]{0,1,2:T(8,128)(2,1)} async-done(((bf16[128,16,64]{0,1,2:T(8,128)(2,1)}), bf16[128,16,256]{0,1,2:T(8,128)(2,1)}) %all-gather.3.cloned.1.call-update) | async-done | bytes 1048592 | tf_op jit(solution)/shard_map/all_gather | solution.py:76
  317.5 17.0 %collective-permute-start = (bf16[128,3,256]{2,0,1:T(8,128)(2,1)S(1)}, bf16[128,3,256]{2,0,1:T(8,128)(2,1)S(1)}, u32[]{:S(2)}, u32[]{:S(2)}) collective-permute-start(bf16[128,3,256]{2,0,1:T(8,128)(2,1)S(1)} %get-tuple-element.29), channel_id=1, source_target_pairs={{0,4},{4,8},{8,12},{12,16},{16,20},{20,24},{24,28},{28,32},{32,36}... | collective-permute-start | bytes 589832 | tf_op jit(solution)/shard_map/ppermute | solution.py:17
  334.5 2.6 collective-permute-done
  337.1 2.8 collective-permute-done.1
  351.9 2.1 fusion.21
  354.0 2.1 convolution_add_fusion.13
  356.1 1.7 convolution_add_fusion.12
  361.1 78.1 %psum.57 = bf16[128,128]{1,0:T(8,128)(2,1)S(1)} all-reduce(f32[128,128]{1,0:T(8,128)S(1)} %fusion.149), channel_id=1, replica_groups=mesh['tiles'=64,'cols'=4] {'tiles','cols'}, use_global_device_ids=true, to_apply=%region_3.7 | all-reduce | flops 16384 | bytes 98304 | tf_op jit(solution)/shard_map/psum | solution.py:85
  440.4 237.6 %all-reduce.8.cloned.1.call-done = f32[128,128]{0,1:T(8,128)} async-done(((f32[128,128]{0,1:T(8,128)}), f32[128,128]{0,1:T(8,128)}) %all-reduce.8.cloned.1.call-update) | async-done | bytes 65552 | tf_op jit(solution)/shard_map/psum | solution.py:27
  679.8 11.7 cholesky.70
  692.9 9.8 custom-call.8
  704.3 20.8 %all-gather.5.cloned.1.call-done = bf16[128,16,256]{0,1,2:T(8,128)(2,1)} async-done(((bf16[128,16,64]{0,1,2:T(8,128)(2,1)}), bf16[128,16,256]{0,1,2:T(8,128)(2,1)}) %all-gather.5.cloned.1.call-update) | async-done | bytes 1048592 | tf_op jit(solution)/shard_map/all_gather | solution.py:76
  726.8 4.0 collective-permute-start.2
  730.8 2.6 collective-permute-done.2
  733.4 2.8 collective-permute-done.3
  738.0 1.6 gather_fusion.8
  748.2 2.1 fusion.12
  750.3 2.1 convolution_add_fusion.6
  752.5 1.7 convolution_add_fusion.5
  757.5 78.5 %all-reduce.11 = bf16[256,128]{1,0:T(8,128)(2,1)S(1)} all-reduce(f32[256,128]{1,0:T(8,128)S(1)} %fusion.56), channel_id=1, replica_groups=mesh['tiles'=64,'cols'=4] {'tiles','cols'}, use_global_device_ids=true, to_apply=%region_5.9 | all-reduce | flops 32768 | bytes 196608 | tf_op jit(solution)/shard_map/psum | solution.py:85
  837.5 237.6 %all-reduce.10.cloned.1.call-done = f32[128,128]{0,1:T(8,128)} async-done(((f32[128,128]{0,1:T(8,128)}), f32[128,128]{0,1:T(8,128)}) %all-reduce.10.cloned.1.call-update) | async-done | bytes 65552 | tf_op jit(solution)/shard_map/psum | solution.py:27
  1076.9 11.7 cholesky.81
  1090.0 9.8 custom-call.9
  1102.1 3.4 all-to-all-start.1
  1105.5 75.5 %all-reduce = (f32[1,128]{1,0:T(1,128)S(1)}, f32[1,128]{1,0:T(1,128)S(1)}, f32[1,128]{1,0:T(1,128)S(1)}) all-reduce(f32[1,128]{1,0:T(1,128)S(1)} %bitcast.212, f32[1,128]{1,0:T(1,128)S(1)} %bitcast.211, f32[1,128]{1,0:T(1,128)S(1)} %bitcast.210), channel_id=1, replica_groups=mesh['tiles'=64,'cols'=4] {'tiles','cols'}, use_global_device_ids=true, to_apply=%region_12.16 | all-reduce | flops 384 | bytes 3072 | tf_op jit(solution)/shard_map/psum | solution.py:39
  (127 shorter events, 55.9 us)
Async XLA Ops:
  11.2 10.4 all-to-all-start
  16.0 252.7 %all-reduce.6.cloned.1.call-start = ((), (), s32[]{:S(2)}) async-start(), calls=%async_computation.2 | async-start | bytes 131072 | tf_op jit(solution)/shard_map/psum | solution.py:27
  22.1 272.9 %copy-start.11 = (s32[16,8]{0,1:T(8,128)S(1)}, s32[16,8]{0,1:T(8,128)}, u32[]{:S(2)}) copy-start(s32[16,8]{0,1:T(8,128)} %param.11) | copy-start | bytes 1540
  24.2 291.6 %all-gather.3.cloned.1.call-start = ((), (), s32[]{:S(2)}) async-start(), calls=%async_computation.3 | async-start | bytes 1310720 | tf_op jit(solution)/shard_map/all_gather | solution.py:76
  294.9 383.1 %all-reduce.8.cloned.1.call-start = ((), (), s32[]{:S(2)}) async-start(), calls=%async_computation.4 | async-start | bytes 131072 | tf_op jit(solution)/shard_map/psum | solution.py:27
  317.5 19.6 %collective-permute-start = (bf16[128,3,256]{2,0,1:T(8,128)(2,1)S(1)}, bf16[128,3,256]{2,0,1:T(8,128)(2,1)S(1)}, u32[]{:S(2)}, u32[]{:S(2)}) collective-permute-start(bf16[128,3,256]{2,0,1:T(8,128)(2,1)S(1)} %get-tuple-element.29), channel_id=1, source_target_pairs={{0,4},{4,8},{8,12},{12,16},{16,20},{20,24},{24,28},{28,32},{32,36}... | collective-permute-start | bytes 589832 | tf_op jit(solution)/shard_map/ppermute | solution.py:17
  334.5 5.4 collective-permute-start.1
  351.9 4.2 copy-start.9
  351.9 6.0 copy-start.8
  351.9 6.0 copy-start.12
  354.0 4.5 copy-start.7
  356.1 2.9 copy-start.6
  357.9 1.7 copy-start.4
  440.3 284.8 %all-gather.5.cloned.1.call-start = ((), (), s32[]{:S(2)}) async-start(), calls=%async_computation.5 | async-start | bytes 1310720 | tf_op jit(solution)/shard_map/all_gather | solution.py:76
  704.3 370.8 %all-reduce.10.cloned.1.call-start = ((), (), s32[]{:S(2)}) async-start(), calls=%async_computation.6 | async-start | bytes 131072 | tf_op jit(solution)/shard_map/psum | solution.py:27
  726.8 6.6 collective-permute-start.2
  730.8 5.4 collective-permute-start.3
  748.2 4.2 copy-start.5
  748.2 6.0 copy-start.3
  748.2 6.0 copy-start.13
  750.3 4.5 copy-start.2
  752.5 2.9 copy-start.1
  754.2 1.7 copy-start
  756.5 80.9 %copy-start.10 = (f32[16,64]{1,0:T(8,128)S(1)}, f32[16,64]{1,0:T(8,128)}, u32[]{:S(2)}) copy-start(f32[16,64]{1,0:T(8,128)} %param.14) | copy-start | bytes 12292
  1102.1 79.5 %all-to-all-start.1 = ((bf16[4,2,16384]{2,1,0:T(2,128)(2,1)}), bf16[4,2,16384]{2,1,0:T(2,128)(2,1)S(1)}, u32[]{:S(2)}, u32[]{:S(2)}) async-start(bf16[4,2,16384]{2,1,0:T(2,128)(2,1)} %reshape.232), calls=%async_computation.1 | async-start | bytes 524288 | tf_op jit(solution)/shard_map/all_to_all | solution.py:100
Sparse Core Ops, SparseCore 0:
  24.4 244.2 all-reduce.5
  295.1 20.7 all-gather.2
  440.5 237.5 all-reduce.7
  704.4 20.7 all-gather.4
  837.5 237.5 all-reduce.9
where the time goes:
time: 1200 us; the launch traced here: 1190 us
  waiting for transfers between devices  776 us (65%)
  blocking collectives  232 us (19%)
  other arithmetic  72.9 us (6%)
  local copies, waits for them, and re-layouts  41.8 us (3%)
  starting transfers between devices  29.4 us (2%)
  matrix products  23 us (2%)
  between operations  14.8 us (1%)
    psum x3, waiting for transfers between devices, orthonormal(): lax.psum(jnp.dot(work, work.T, preferred_element_type=jnp.float32), ('til...  719 us
    psum x2, blocking collectives, local(): sums = lax.psum(local_sums, ('tiles', 'cols'))  157 us
    psum x1, blocking collectives, settle(): return lax.psum(terms, ('tiles', 'cols'))  75.5 us
    all_gather x2, waiting for transfers between devices, local(): gathered = lax.all_gather(basis_cube, 'cols', axis=2, tiled=True)  41.6 us
    another operation x9, other arithmetic, orthonormal(): lower = jnp.linalg.cholesky(gram)  37.2 us
    another operation x6, other arithmetic, orthonormal(): jax.scipy.linalg.solve_triangular(lower, identity, lower=True)  31.4 us
  transfers between devices with their start and end apart: 11, of which 10 were waited for; matrix products, arithmetic and copies ran while one was open for 0% of the time, Pallas kernels for 0%

commit v1 on v0

--- a/solution.py
+++ b/solution.py
@@ -82,7 +82,8 @@
         else:
             stacked = jnp.concatenate([basis_now, basis_old], axis=0)
         local_sums = jnp.dot(stacked, image.T, preferred_element_type=jnp.float32)
-        sums = lax.psum(local_sums, ("tiles", "cols"))
+        parts = lax.all_gather(local_sums, ("tiles", "cols"), axis=0, tiled=False)
+        sums = parts.sum(axis=0)
         along = sums[:count].astype(jnp.bfloat16)
         resid = image.astype(jnp.float32) - jnp.dot(
             along.T, basis_now, preferred_element_type=jnp.float32

time: 1200 us -> 1340 us (1.12)
  waiting for transfers between devices: 776 us -> 1060 us
  blocking collectives: 232 us -> 75.5 us
  other arithmetic: 72.9 us -> 91.7 us
    all_gather x0 -> x2, waiting for transfers between devices: none -> 277 us  [local(): parts = lax.all_gather(local_sums, ('tiles', 'cols'), axis=0, tiled=False)]
    psum x2 -> x0, blocking collectives: 157 us -> none  [local(): sums = lax.psum(local_sums, ('tiles', 'cols'))]
    reduce_sum x0 -> x2, other arithmetic: none -> 18.8 us  [local(): sums = parts.sum(axis=0)]
  transfers between devices with their start and end apart: 11 -> 13, of which waited for: 10 -> 12; matrix products, arithmetic and copies ran while one was open for 0% -> 0% of each run, Pallas kernels for 0% -> 0%
where the time goes in v1:
time: 1340 us; the launch traced here: 1330 us
  waiting for transfers between devices  1060 us (79%)
  other arithmetic  91.7 us (7%)
  blocking collectives  75.5 us (6%)
  local copies, waits for them, and re-layouts  41.8 us (3%)
  starting transfers between devices  29.6 us (2%)
  matrix products  24.2 us (2%)
  between operations  15.1 us (1%)
    psum x3, waiting for transfers between devices, orthonormal(): lax.psum(jnp.dot(work, work.T, preferred_element_type=jnp.float32), ('til...  721 us
    all_gather x2, waiting for transfers between devices, local(): parts = lax.all_gather(local_sums, ('tiles', 'cols'), axis=0, tiled=False)  277 us
    psum x1, blocking collectives, settle(): return lax.psum(terms, ('tiles', 'cols'))  75.5 us
    all_gather x2, waiting for transfers between devices, local(): gathered = lax.all_gather(basis_cube, 'cols', axis=2, tiled=True)  41.6 us
    another operation x9, other arithmetic, orthonormal(): lower = jnp.linalg.cholesky(gram)  37.2 us
    another operation x6, other arithmetic, orthonormal(): jax.scipy.linalg.solve_triangular(lower, identity, lower=True)  31.4 us
  transfers between devices with their start and end apart: 13, of which 12 were waited for; matrix products, arithmetic and copies ran while one was open for 0% of the time, Pallas kernels for 0%

profile of v1, /device:TPU:1, one launch (start us, length us, event | category | flops | bytes accessed | tf_op | source)
XLA Modules:
  0.0 1333.8 jit_solution(14685793195251824897)
XLA Ops:
  7.2 2.4 copy.138
  11.2 4.8 all-to-all-start
  16.7 4.8 all-to-all-done
  24.7 244.1 %all-reduce.5.cloned.1.call-done = f32[128,128]{0,1:T(8,128)} async-done(((f32[128,128]{0,1:T(8,128)}), f32[128,128]{0,1:T(8,128)}) %all-reduce.5.cloned.1.call-update) | async-done | bytes 65552 | tf_op jit(solution)/shard_map/psum | solution.py:27
  270.5 11.7 cholesky.59
  283.6 9.8 custom-call.7
  295.1 20.7 %all-gather.7.cloned.1.call-done = bf16[128,16,256]{0,1,2:T(8,128)(2,1)} async-done(((bf16[128,16,64]{0,1,2:T(8,128)(2,1)}), bf16[128,16,256]{0,1,2:T(8,128)(2,1)}) %all-gather.7.cloned.1.call-update) | async-done | bytes 1048592 | tf_op jit(solution)/shard_map/all_gather | solution.py:76
  317.5 16.9 %collective-permute-start = (bf16[128,3,256]{2,0,1:T(8,128)(2,1)S(1)}, bf16[128,3,256]{2,0,1:T(8,128)(2,1)S(1)}, u32[]{:S(2)}, u32[]{:S(2)}) collective-permute-start(bf16[128,3,256]{2,0,1:T(8,128)(2,1)S(1)} %get-tuple-element.29), channel_id=1, source_target_pairs={{0,4},{4,8},{8,12},{12,16},{16,20},{20,24},{24,28},{28,32},{32,36}... | collective-permute-start | bytes 589832 | tf_op jit(solution)/shard_map/ppermute | solution.py:17
  334.5 2.6 collective-permute-done
  337.1 2.8 collective-permute-done.1
  351.9 2.1 fusion.21
  354.0 2.1 convolution_add_fusion.13
  356.2 1.7 convolution_add_fusion.12
  361.8 125.4 %all-gather.11.cloned.1.call-done = f32[32768,128]{1,0:T(8,128)} async-done(((f32[128,128]{1,0:T(8,128)}), f32[32768,128]{1,0:T(8,128)}) %all-gather.11.cloned.1.call-update) | async-done | bytes 16777232 | tf_op jit(solution)/shard_map/all_gather | solution.py:85
  487.2 6.6 reduce_sum.45
  495.0 238.6 %all-reduce.7.cloned.1.call-done = f32[128,128]{0,1:T(8,128)} async-done(((f32[128,128]{0,1:T(8,128)}), f32[128,128]{0,1:T(8,128)}) %all-reduce.7.cloned.1.call-update) | async-done | bytes 65552 | tf_op jit(solution)/shard_map/psum | solution.py:27
  735.4 11.7 cholesky.70
  748.5 9.8 custom-call.8
  759.9 20.8 %all-gather.9.cloned.1.call-done = bf16[128,16,256]{0,1,2:T(8,128)(2,1)} async-done(((bf16[128,16,64]{0,1,2:T(8,128)(2,1)}), bf16[128,16,256]{0,1,2:T(8,128)(2,1)}) %all-gather.9.cloned.1.call-update) | async-done | bytes 1048592 | tf_op jit(solution)/shard_map/all_gather | solution.py:76
  782.4 4.0 collective-permute-start.2
  786.4 2.6 collective-permute-done.2
  789.0 2.8 collective-permute-done.3
  803.9 2.1 fusion.12
  805.9 2.1 convolution_add_fusion.6
  808.1 1.7 convolution_add_fusion.5
  814.0 152.1 %all-gather.13.cloned.1.call-done = f32[65536,128]{1,0:T(8,128)} async-done(((f32[256,128]{1,0:T(8,128)}), f32[65536,128]{1,0:T(8,128)}) %all-gather.13.cloned.1.call-update) | async-done | bytes 33554448 | tf_op jit(solution)/shard_map/all_gather | solution.py:85
  966.1 12.2 reduce_sum.46
  979.8 238.5 %all-reduce.9.cloned.1.call-done = f32[128,128]{0,1:T(8,128)} async-done(((f32[128,128]{0,1:T(8,128)}), f32[128,128]{0,1:T(8,128)}) %all-reduce.9.cloned.1.call-update) | async-done | bytes 65552 | tf_op jit(solution)/shard_map/psum | solution.py:27
  1220.1 11.7 cholesky.81
  1233.1 9.8 custom-call.9
  1245.3 3.4 all-to-all-start.1
  1248.7 75.5 %all-reduce = (f32[1,128]{1,0:T(1,128)S(1)}, f32[1,128]{1,0:T(1,128)S(1)}, f32[1,128]{1,0:T(1,128)S(1)}) all-reduce(f32[1,128]{1,0:T(1,128)S(1)} %bitcast.216, f32[1,128]{1,0:T(1,128)S(1)} %bitcast.215, f32[1,128]{1,0:T(1,128)S(1)} %bitcast.214), channel_id=1, replica_groups=mesh['tiles'=64,'cols'=4] {'tiles','cols'}, use_global_device_ids=true, to_apply=%region_12.16 | all-reduce | flops 384 | bytes 3072 | tf_op jit(solution)/shard_map/psum | solution.py:39
  (133 shorter events, 60.7 us)
Async XLA Ops:
  11.2 10.4 all-to-all-start
  16.0 252.7 %all-reduce.5.cloned.1.call-start = ((), (), s32[]{:S(2)}) async-start(), calls=%async_computation.2 | async-start | bytes 131072 | tf_op jit(solution)/shard_map/psum | solution.py:27
  22.1 273.0 %copy-start.11 = (s32[16,8]{0,1:T(8,128)S(1)}, s32[16,8]{0,1:T(8,128)}, u32[]{:S(2)}) copy-start(s32[16,8]{0,1:T(8,128)} %param.11) | copy-start | bytes 1540
  24.2 291.6 %all-gather.7.cloned.1.call-start = ((), (), s32[]{:S(2)}) async-start(), calls=%async_computation.3 | async-start | bytes 1310720 | tf_op jit(solution)/shard_map/all_gather | solution.py:76
  295.0 192.2 %all-gather.11.cloned.1.call-start = ((), (), s32[]{:S(2)}) async-start(), calls=%async_computation.7 | async-start | bytes 16842752 | tf_op jit(solution)/shard_map/all_gather | solution.py:85
  317.5 19.5 %collective-permute-start = (bf16[128,3,256]{2,0,1:T(8,128)(2,1)S(1)}, bf16[128,3,256]{2,0,1:T(8,128)(2,1)S(1)}, u32[]{:S(2)}, u32[]{:S(2)}) collective-permute-start(bf16[128,3,256]{2,0,1:T(8,128)(2,1)S(1)} %get-tuple-element.29), channel_id=1, source_target_pairs={{0,4},{4,8},{8,12},{12,16},{16,20},{20,24},{24,28},{28,32},{32,36}... | collective-permute-start | bytes 589832 | tf_op jit(solution)/shard_map/ppermute | solution.py:17
  334.5 5.4 collective-permute-start.1
  351.9 4.3 copy-start.9
  351.9 6.0 copy-start.8
  351.9 6.0 copy-start.12
  354.0 4.5 copy-start.7
  356.2 2.9 copy-start.6
  357.9 1.7 copy-start.4
  361.6 372.0 %all-reduce.7.cloned.1.call-start = ((), (), s32[]{:S(2)}) async-start(), calls=%async_computation.4 | async-start | bytes 131072 | tf_op jit(solution)/shard_map/psum | solution.py:27
  494.9 285.8 %all-gather.9.cloned.1.call-start = ((), (), s32[]{:S(2)}) async-start(), calls=%async_computation.5 | async-start | bytes 1310720 | tf_op jit(solution)/shard_map/all_gather | solution.py:76
  759.9 206.2 %all-gather.13.cloned.1.call-start = ((), (), s32[]{:S(2)}) async-start(), calls=%async_computation.8 | async-start | bytes 33685504 | tf_op jit(solution)/shard_map/all_gather | solution.py:85
  782.4 6.6 collective-permute-start.2
  786.4 5.4 collective-permute-start.3
  803.8 4.2 copy-start.5
  803.8 6.0 copy-start.3
  803.9 6.0 copy-start.13
  805.9 4.5 copy-start.2
  808.1 2.9 copy-start.1
  809.8 1.7 copy-start
  813.7 404.6 %all-reduce.9.cloned.1.call-start = ((), (), s32[]{:S(2)}) async-start(), calls=%async_computation.6 | async-start | bytes 131072 | tf_op jit(solution)/shard_map/psum | solution.py:27
  966.1 13.6 %copy-start.10 = (f32[16,64]{1,0:T(8,128)S(1)}, f32[16,64]{1,0:T(8,128)}, u32[]{:S(2)}) copy-start(f32[16,64]{1,0:T(8,128)} %param.14) | copy-start | bytes 12292
  1245.3 79.5 %all-to-all-start.1 = ((bf16[4,2,16384]{2,1,0:T(2,128)(2,1)}), bf16[4,2,16384]{2,1,0:T(2,128)(2,1)S(1)}, u32[]{:S(2)}, u32[]{:S(2)}) async-start(bf16[4,2,16384]{2,1,0:T(2,128)(2,1)} %reshape.234), calls=%async_computation.1 | async-start | bytes 524288 | tf_op jit(solution)/shard_map/all_to_all | solution.py:101
Sparse Core Ops, SparseCore 0:
  24.4 244.3 all-reduce.4
  295.1 20.7 all-gather.6
  361.7 125.4 all-gather.10
  495.1 238.5 all-reduce.6
  760.0 20.7 all-gather.8
  813.8 152.2 all-gather.12
  979.9 238.3 all-reduce.8
